TPU v7x, 128 devices: a whole 4x4x4 slice. The times are simulated.
128 devices in a mesh: group: 2 (over core), member: 64 (over x, z, y).
Axes of the slice: x: 4, y: 4, z: 4, core: 2. Of those that a mesh axis runs over, the one named last changes fastest.
Arguments:
- features: bfloat16 [262144, 256], P(('group', 'member')), may hold values from -6 to 6
- local_home: int32 [8192], P(('group', 'member')), may hold values from 0 to 15
- local_near: int32 [8192], P(('group', 'member')), may hold values from 0 to 15
- local_tiles: bfloat16 [8192, 128, 128], P(('group', 'member')), may hold values from -0.125 to 0.125
- remote_home: int32 [8192], P(('group', 'member')), may hold values from 0 to 15
- remote_far: int32 [8192], P(('group', 'member')), may hold values from 0 to 2047, as said below
- remote_tiles: bfloat16 [8192, 128, 128], P(('group', 'member')), may hold values from -0.125 to 0.125
- weight: bfloat16 [512, 256], replicated, may hold values from -0.25 to 0.25
- cotangent: bfloat16 [262144, 256], P(('group', 'member')), may hold values from -6 to 6
Outputs:
- output: bfloat16 [262144, 256], P(('group', 'member'))
- grad_weight: float32 [512, 256], replicated
- grad_features: float32 [262144, 256], P(('group', 'member'))
Inputs may be any that keep to these rules, and one draw needn't show every extreme that they name: `remote_far`: the remote pairs of one owner name partner blocks on 64 different owners other than itself, one block from each owner; one owner, drawn from the seed, holds a partner block of every other owner's remote pairs.
All inputs are finite; a program needn't handle non-finite values.
Results may differ from a plain program's by a relative error of at most 0.0057.
Values may be sent and summed in bfloat16 or wider, within the bound.
No kernel may reach another device: no remote copies, remote signals or barrier semaphores. Data moves between devices by JAX's collectives and lax.ppermute only.
A program may use at most 192 MiB of HBM per device.

v0:
```python
import math
import jax
import jax.numpy as jnp
from jax import lax
from jax.sharding import PartitionSpec as P

F = 256
BLOCK = 128
BLK_DEV = 16


def spread(index_list, count, dtype):
    return (index_list[:, None] == jnp.arange(count, dtype=jnp.int32)[None, :]).astype(dtype)


def carry_blocks(buffer):
    return lax.all_to_all(buffer, ("group", "member"), split_axis=0, concat_axis=0, tiled=True)


def return_blocks(buffer):
    return lax.all_to_all(buffer, ("group", "member"), split_axis=0, concat_axis=0, tiled=True)


def body(
    features,
    local_home,
    local_near,
    local_tiles,
    remote_home,
    remote_far,
    remote_tiles,
    weight,
    cotangent,
):
    device_count = lax.axis_size(("group", "member"))
    row_count = features.shape[0]
    own_blocks = row_count // BLOCK
    target_dev = remote_far // BLK_DEV
    wanted = remote_far % BLK_DEV
    request = jnp.full((device_count,), -1, jnp.int32).at[target_dev].set(wanted)
    asked = lax.all_to_all(request, ("group", "member"), split_axis=0, concat_axis=0, tiled=True)
    picked = jnp.clip(asked, 0, own_blocks - 1)
    back_hot = spread(asked, own_blocks, jnp.bfloat16)
    segment_ids = jnp.concatenate([local_home, local_near, remote_home])

    def apply_graph(blocks_in):
        outgoing = blocks_in[picked]
        arrived = carry_blocks(outgoing)
        to_far = jnp.einsum(
            "pba,pbf->paf", remote_tiles, blocks_in[remote_home], preferred_element_type=jnp.float32
        ).astype(jnp.bfloat16)
        send_back = jnp.zeros((device_count, BLOCK, F), jnp.bfloat16).at[target_dev].set(to_far)
        returned = return_blocks(send_back)
        to_home = jnp.einsum(
            "pab,pbf->paf", local_tiles, blocks_in[local_near], preferred_element_type=jnp.float32
        )
        to_near = jnp.einsum(
            "pba,pbf->paf", local_tiles, blocks_in[local_home], preferred_element_type=jnp.float32
        )
        far_vals = arrived[target_dev]
        to_home_r = jnp.einsum(
            "pab,pbf->paf", remote_tiles, far_vals, preferred_element_type=jnp.float32
        )
        products = jnp.concatenate([to_home, to_near, to_home_r], axis=0)
        total = jax.ops.segment_sum(products, segment_ids, num_segments=own_blocks)
        total = total + jnp.einsum(
            "sk,saf->kaf", back_hot, returned, preferred_element_type=jnp.float32
        )
        return total.reshape(row_count, F)

    aggregate = apply_graph(features.reshape(own_blocks, BLOCK, F)).astype(jnp.bfloat16)
    joined = jnp.concatenate([features, aggregate], axis=1)
    pre_act = jnp.dot(joined, weight, preferred_element_type=jnp.float32)
    sigmoid_z = jax.nn.sigmoid(pre_act)
    output = (pre_act * sigmoid_z).astype(jnp.bfloat16)
    grad_pre = (
        cotangent.astype(jnp.float32) * sigmoid_z * (1.0 + pre_act * (1.0 - sigmoid_z))
    ).astype(jnp.bfloat16)
    partial_grad = jnp.einsum("ra,rf->af", joined, grad_pre, preferred_element_type=jnp.float32)
    grad_scale = 1.0 / math.sqrt(row_count * device_count)
    grad_weight = lax.psum(partial_grad, ("group", "member")) * grad_scale
    grad_joined = jnp.einsum("rf,af->ra", grad_pre, weight, preferred_element_type=jnp.float32)
    grad_agg = grad_joined[:, F:].astype(jnp.bfloat16).reshape(own_blocks, BLOCK, F)
    grad_features = grad_joined[:, :F] + apply_graph(grad_agg)
    return (output, grad_weight, grad_features)


def solution(mesh):
    in_specs = (
        P(("group", "member"), None),
        P(("group", "member")),
        P(("group", "member")),
        P(("group", "member"), None, None),
        P(("group", "member")),
        P(("group", "member")),
        P(("group", "member"), None, None),
        P(),
        P(("group", "member"), None),
    )
    out_specs = (P(("group", "member"), None), P(), P(("group", "member"), None))
    return jax.shard_map(body, mesh=mesh, in_specs=in_specs, out_specs=out_specs, check_vma=False)
```

profile of v0, /device:TPU:1, one launch (start us, length us, event | category | flops | bytes accessed | tf_op | source)
XLA Modules:
  0.0 955.4 jit_solution(5109169967945188336)
XLA Ops:
  7.2 0.0 copy-start
  7.2 0.8 and_select_fusion
  8.0 0.8 scatter_custom_fusion
  8.8 0.7 copy.50
  9.5 11.5 %all-to-all-start = ((s32[128,1,1]{2,1,0:T(1,128)}), s32[128,1,1]{2,1,0:T(1,128)S(1)}, u32[]{:S(2)}, u32[]{:S(2)}) async-start(s32[128,1,1]{2,1,0:T(1,128)} %copy.50), calls=%async_computation | async-start | bytes 131072 | tf_op jit(solution)/shard_map/all_to_all | solution.py:41
  21.0 0.7 compare_select_fusion.3
  21.7 4.0 gather_fusion
  25.7 6.1 convert_bitcast_fusion.1
  31.8 6.4 copy.52
  38.2 4.3 broadcast.61.clone
  42.4 12.0 %scatter_fusion = bf16[128,128,256]{2,1,0:T(8,128)(2,1)} fusion(bf16[128,128,256]{2,1,0:T(8,128)(2,1)} %broadcast.61.clone, s32[64]{0:T(128)S(1)} %get-tuple-element.8, bf16[64,128,256]{2,1,0:T(8,128)(2,1)} %copy.52), kind=kCustom, calls=%fused_computation.11 | custom fusion | bytes 12583168 | tf_op jit(solution)/shard_map/scatter | solution.py:52
  54.5 10.3 %all-to-all-start.1 = ((bf16[128,128,256]{2,1,0:T(8,128)(2,1)}), bf16[128,128,256]{2,1,0:T(8,128)(2,1)}, u32[]{:S(2)}, u32[]{:S(2)}) async-start(bf16[128,128,256]{2,1,0:T(8,128)(2,1)} %scatter_fusion), calls=%async_computation.1 | async-start | bytes 16777216 | tf_op jit(solution)/shard_map/all_to_all | solution.py:21
  64.8 4.6 clamp_reduce_fusion
  69.4 6.5 gather_fusion.3
  75.9 100.2 %all-to-all-done.1 = bf16[128,128,256]{2,1,0:T(8,128)(2,1)} async-done(((bf16[128,128,256]{2,1,0:T(8,128)(2,1)}), bf16[128,128,256]{2,1,0:T(8,128)(2,1)}, u32[]{:S(2)}, u32[]{:S(2)}) %all-to-all-start.1) | async-done | bytes 8388640 | tf_op jit(solution)/shard_map/all_to_all | solution.py:21
  176.1 15.4 %all-to-all-start.2 = ((bf16[128,128,256]{2,1,0:T(8,128)(2,1)}), bf16[128,128,256]{2,1,0:T(8,128)(2,1)}, u32[]{:S(2)}, u32[]{:S(2)}) async-start(bf16[128,128,256]{2,1,0:T(8,128)(2,1)} %gather_fusion.3), calls=%async_computation.2 | async-start | bytes 16777216 | tf_op jit(solution)/shard_map/all_to_all | solution.py:17
  191.6 0.0 copy-start.9
  191.6 2.9 gather_fusion.2
  194.5 0.0 copy-start.8
  194.5 2.8 gather_fusion.1
  197.3 0.1 pad_add_fusion
  197.4 6.9 convolution_bitcast_fusion.4
  204.2 4.5 convolution_bitcast_fusion.5
  208.8 7.9 fusion.2
  216.7 2.5 copy.57
  219.2 82.9 %all-to-all-done.2 = bf16[128,128,256]{2,1,0:T(8,128)(2,1)} async-done(((bf16[128,128,256]{2,1,0:T(8,128)(2,1)}), bf16[128,128,256]{2,1,0:T(8,128)(2,1)}, u32[]{:S(2)}, u32[]{:S(2)}) %all-to-all-start.2) | async-done | bytes 8388640 | tf_op jit(solution)/shard_map/all_to_all | solution.py:17
  302.1 6.1 gather_fusion.4
  308.2 4.2 convolution_bitcast_fusion.3
  312.4 15.8 %pad_maximum_fusion = f32[192,128,256]{1,2,0:T(8,128)} fusion(f32[64,128,256]{1,2,0:T(8,128)S(1)} %convolution_bitcast_fusion.3, f32[64,128,256]{1,2,0:T(8,128)} %convolution_bitcast_fusion.4, f32[64,128,256]{1,2,0:T(8,128)} %convolution_bitcast_fusion.5), kind=kLoop, calls=%fused_computation.15 | loop fusion | flops 12582912 | bytes 50331648 | tf_op jit(solution)/shard_map/concatenate | solution.py:64
  328.2 24.6 %copy.58 = f32[192,128,256]{2,1,0:T(8,128)} copy(f32[192,128,256]{1,2,0:T(8,128)} %pad_maximum_fusion) | data formatting | bytes 50331648 | tf_op jit(solution)/shard_map/concatenate | solution.py:64
  352.8 55.2 %scatter_fusion.1 = f32[16,128,256]{2,1,0:T(8,128)} fusion(f32[16,128,256]{2,1,0:T(8,128)} %copy.57, s32[192]{0:T(256)S(1)} %pad_add_fusion, f32[192,128,256]{2,1,0:T(8,128)} %copy.58), kind=kCustom, calls=%fused_computation.12 | custom fusion | flops 6291456 | bytes 75498240 | tf_op jit(solution)/shard_map/scatter-add | solution.py:65
  408.0 1.7 convert_element_type.31
  409.8 3.9 multiply_convert_fusion
  413.7 0.7 fusion.16
  414.4 0.2 copy-done.5
  414.6 2.0 copy-done.2
  416.7 0.1 slice.33
  416.8 2.8 gather_fusion.5
  419.6 6.1 convert_bitcast_fusion
  425.7 6.4 copy.60
  432.1 4.3 broadcast.61
  436.4 12.0 %scatter_fusion.2 = bf16[128,128,256]{2,1,0:T(8,128)(2,1)} fusion(bf16[128,128,256]{2,1,0:T(8,128)(2,1)} %broadcast.61, s32[64]{0:T(128)S(1)} %get-tuple-element.8, bf16[64,128,256]{2,1,0:T(8,128)(2,1)} %copy.60), kind=kCustom, calls=%fused_computation.13 | custom fusion | bytes 12583168 | tf_op jit(solution)/shard_map/scatter | solution.py:52
  448.4 15.1 %all-to-all-start.3 = ((bf16[128,128,256]{2,1,0:T(8,128)(2,1)}), bf16[128,128,256]{2,1,0:T(8,128)(2,1)}, u32[]{:S(2)}, u32[]{:S(2)}) async-start(bf16[128,128,256]{2,1,0:T(8,128)(2,1)} %scatter_fusion.2), calls=%async_computation.3 | async-start | bytes 16777216 | tf_op jit(solution)/shard_map/all_to_all | solution.py:21
  463.4 6.5 gather_fusion.8
  469.9 104.9 %all-to-all-done.3 = bf16[128,128,256]{2,1,0:T(8,128)(2,1)} async-done(((bf16[128,128,256]{2,1,0:T(8,128)(2,1)}), bf16[128,128,256]{2,1,0:T(8,128)(2,1)}, u32[]{:S(2)}, u32[]{:S(2)}) %all-to-all-start.3) | async-done | bytes 8388640 | tf_op jit(solution)/shard_map/all_to_all | solution.py:21
  574.8 15.1 %all-to-all-start.4 = ((bf16[128,128,256]{2,1,0:T(8,128)(2,1)}), bf16[128,128,256]{2,1,0:T(8,128)(2,1)}, u32[]{:S(2)}, u32[]{:S(2)}) async-start(bf16[128,128,256]{2,1,0:T(8,128)(2,1)} %gather_fusion.8), calls=%async_computation.4 | async-start | bytes 16777216 | tf_op jit(solution)/shard_map/all_to_all | solution.py:17
  589.9 0.3 all-reduce.2.cloned.1.call-start
  590.2 2.9 gather_fusion.7
  593.0 2.8 gather_fusion.6
  595.8 3.4 fusion.4
  599.2 0.0 all-reduce.2.cloned.1.call-update
  599.3 6.9 convolution_bitcast_fusion.1
  606.1 4.5 convolution_bitcast_fusion.2
  610.6 215.4 %all-reduce.2.cloned.1.call-done = f32[512,256]{1,0:T(8,128)} async-done(((f32[512,256]{1,0:T(8,128)}), f32[512,256]{1,0:T(8,128)}) %all-reduce.2.cloned.1.call-update) | async-done | bytes 524304 | tf_op jit(solution)/shard_map/psum | solution.py:81
  826.0 1.9 broadcast_multiply_fusion
  827.9 7.9 fusion
  835.8 2.5 copy.65
  838.3 0.0 all-to-all-done.4
  838.3 6.1 gather_fusion.9
  844.4 4.2 convolution_bitcast_fusion
  848.6 15.8 %pad_maximum_fusion.1 = f32[192,128,256]{1,2,0:T(8,128)} fusion(f32[64,128,256]{1,2,0:T(8,128)S(1)} %convolution_bitcast_fusion, f32[64,128,256]{1,2,0:T(8,128)} %convolution_bitcast_fusion.1, f32[64,128,256]{1,2,0:T(8,128)} %convolution_bitcast_fusion.2), kind=kLoop, calls=%fused_computation.16 | loop fusion | flops 12582912 | bytes 50331648 | tf_op jit(solution)/shard_map/concatenate | solution.py:64
  864.4 24.6 %copy.66 = f32[192,128,256]{2,1,0:T(8,128)} copy(f32[192,128,256]{1,2,0:T(8,128)} %pad_maximum_fusion.1) | data formatting | bytes 50331648 | tf_op jit(solution)/shard_map/concatenate | solution.py:64
  889.0 55.3 %scatter_fusion.3 = f32[16,128,256]{2,1,0:T(8,128)} fusion(f32[16,128,256]{2,1,0:T(8,128)} %copy.65, s32[192]{0:T(256)S(1)} %pad_add_fusion, f32[192,128,256]{2,1,0:T(8,128)} %copy.66), kind=kCustom, calls=%fused_computation.14 | custom fusion | flops 6291456 | bytes 75498240 | tf_op jit(solution)/shard_map/scatter-add | solution.py:65
  944.3 3.8 slice_add_fusion
  (26 shorter events, 0.1 us)
Async XLA Ops:
  7.2 190.2 %copy-start = (bf16[64,128,128]{2,1,0:T(8,128)(2,1)S(1)}, bf16[64,128,128]{2,1,0:T(8,128)(2,1)}, u32[]{:S(2)}) copy-start(bf16[64,128,128]{2,1,0:T(8,128)(2,1)} %param.12) | copy-start | bytes 6291460
  9.5 44.9 %all-to-all-start = ((s32[128,1,1]{2,1,0:T(1,128)}), s32[128,1,1]{2,1,0:T(1,128)S(1)}, u32[]{:S(2)}, u32[]{:S(2)}) async-start(s32[128,1,1]{2,1,0:T(1,128)} %copy.50), calls=%async_computation | async-start | bytes 131072 | tf_op jit(solution)/shard_map/all_to_all | solution.py:41
  54.5 14.9 %copy-start.1 = (bf16[2048,256]{1,0:T(8,128)(2,1)S(1)}, bf16[2048,256]{1,0:T(8,128)(2,1)}, u32[]{:S(2)}) copy-start(bf16[2048,256]{1,0:T(8,128)(2,1)} %param.9) | copy-start | bytes 3145732
  54.5 121.7 %all-to-all-start.1 = ((bf16[128,128,256]{2,1,0:T(8,128)(2,1)}), bf16[128,128,256]{2,1,0:T(8,128)(2,1)}, u32[]{:S(2)}, u32[]{:S(2)}) async-start(bf16[128,128,256]{2,1,0:T(8,128)(2,1)} %scatter_fusion), calls=%async_computation.1 | async-start | bytes 16777216 | tf_op jit(solution)/shard_map/all_to_all | solution.py:21
  75.9 115.7 %copy-start.10 = (s32[64]{0:T(128)S(1)}, s32[64]{0:T(128)}, u32[]{:S(2)}) copy-start(s32[64]{0:T(128)} %param.10) | copy-start | bytes 772
  176.1 125.9 %all-to-all-start.2 = ((bf16[128,128,256]{2,1,0:T(8,128)(2,1)}), bf16[128,128,256]{2,1,0:T(8,128)(2,1)}, u32[]{:S(2)}, u32[]{:S(2)}) async-start(bf16[128,128,256]{2,1,0:T(8,128)(2,1)} %gather_fusion.3), calls=%async_computation.2 | async-start | bytes 16777216 | tf_op jit(solution)/shard_map/all_to_all | solution.py:17
  191.6 2.9 copy-start.9
  194.5 2.8 copy-start.8
  197.4 6.9 copy-start.4
  352.8 57.0 %copy-start.7 = (bf16[512,256]{1,0:T(8,128)(2,1)S(1)}, bf16[512,256]{1,0:T(8,128)(2,1)}, u32[]{:S(2)}) copy-start(bf16[512,256]{1,0:T(8,128)(2,1)} %param.16) | copy-start | bytes 786436
  409.8 3.9 copy-start.6
  413.7 1.0 copy-start.5
  414.6 2.0 copy-start.2
  448.4 126.5 %all-to-all-start.3 = ((bf16[128,128,256]{2,1,0:T(8,128)(2,1)}), bf16[128,128,256]{2,1,0:T(8,128)(2,1)}, u32[]{:S(2)}, u32[]{:S(2)}) async-start(bf16[128,128,256]{2,1,0:T(8,128)(2,1)} %scatter_fusion.2), calls=%async_computation.3 | async-start | bytes 16777216 | tf_op jit(solution)/shard_map/all_to_all | solution.py:21
  574.8 263.5 %all-to-all-start.4 = ((bf16[128,128,256]{2,1,0:T(8,128)(2,1)}), bf16[128,128,256]{2,1,0:T(8,128)(2,1)}, u32[]{:S(2)}, u32[]{:S(2)}) async-start(bf16[128,128,256]{2,1,0:T(8,128)(2,1)} %gather_fusion.8), calls=%async_computation.4 | async-start | bytes 16777216 | tf_op jit(solution)/shard_map/all_to_all | solution.py:17
  589.9 236.1 %all-reduce.2.cloned.1.call-start = ((), (), s32[]{:S(2)}) async-start(), calls=%async_computation.5 | async-start | bytes 1048576 | tf_op jit(solution)/shard_map/psum | solution.py:81
  599.2 6.9 copy-start.3
Sparse Core Ops, SparseCore 0:
  599.4 226.6 all-reduce.1
where the time goes:
time: 965 us; the launch traced here: 955 us
  waiting for transfers between devices  503 us (52%)
  other arithmetic  156 us (16%)
  local copies, waits for them, and re-layouts  147 us (15%)
  starting transfers between devices  67.6 us (7%)
  matrix products  67.2 us (7%)
  between operations  14.7 us (2%)
    psum x1, waiting for transfers between devices, body(): grad_weight = lax.psum(partial_grad, ('group', 'member')) * grad_scale  215 us
    all_to_all x2, waiting for transfers between devices, return_blocks(): lax.all_to_all(buffer, ('group', 'member'), split_axis=0, concat_axis=0,...  205 us
    scatter-add x2, other arithmetic, apply_graph(): total = jax.ops.segment_sum(products, segment_ids, num_segments=own_blocks)  110 us
    all_to_all x2, waiting for transfers between devices, carry_blocks(): lax.all_to_all(buffer, ('group', 'member'), split_axis=0, concat_axis=0,...  82.9 us
    concatenate x2, local copies, waits for them, and re-layouts, apply_graph(): products = jnp.concatenate([to_home, to_near, to_home_r], axis=0)  49.3 us
    concatenate x2, other arithmetic, apply_graph(): products = jnp.concatenate([to_home, to_near, to_home_r], axis=0)  31.5 us
    all_to_all x2, starting transfers between devices, carry_blocks(): lax.all_to_all(buffer, ('group', 'member'), split_axis=0, concat_axis=0,...  30.5 us
    all_to_all x2, starting transfers between devices, return_blocks(): lax.all_to_all(buffer, ('group', 'member'), split_axis=0, concat_axis=0,...  25.4 us
  transfers between devices with their start and end apart: 6, of which 4 were waited for; matrix products, arithmetic and copies ran while one was open for 12% of the time, Pallas kernels for 0%

commit v1 on v0

--- a/solution.py
+++ b/solution.py
@@ -78,7 +78,7 @@
     ).astype(jnp.bfloat16)
     partial_grad = jnp.einsum("ra,rf->af", joined, grad_pre, preferred_element_type=jnp.float32)
     grad_scale = 1.0 / math.sqrt(row_count * device_count)
-    grad_weight = lax.psum(partial_grad, ("group", "member")) * grad_scale
+    grad_weight = jnp.sum(lax.all_gather(partial_grad, ("group", "member")), axis=0) * grad_scale
     grad_joined = jnp.einsum("rf,af->ra", grad_pre, weight, preferred_element_type=jnp.float32)
     grad_agg = grad_joined[:, F:].astype(jnp.bfloat16).reshape(own_blocks, BLOCK, F)
     grad_features = grad_joined[:, :F] + apply_graph(grad_agg)

time: 965 us -> 883 us (0.915)
  waiting for transfers between devices: 503 us -> 400 us
  other arithmetic: 156 us -> 173 us
    psum x1 -> x0, waiting for transfers between devices: 215 us -> none  [body(): grad_weight = lax.psum(partial_grad, ('group', 'member')) * grad_scale]
    all_to_all x2, waiting for transfers between devices: 82.9 us -> 182 us  [carry_blocks(): lax.all_to_all(buffer, ('group', 'member'), split_axis=0, concat_axis=0,...]
    reduce_sum x0 -> x1, other arithmetic: none -> 20.9 us  [body(): jnp.sum(lax.all_gather(partial_grad, ('group', 'member')), axis=0)]
    all_to_all x2, waiting for transfers between devices: 205 us -> 217 us  [return_blocks(): lax.all_to_all(buffer, ('group', 'member'), split_axis=0, concat_axis=0,...]
  transfers between devices with their start and end apart: 6 -> 6, of which waited for: 4 -> 4; matrix products, arithmetic and copies ran while one was open for 12% -> 28% of each run, Pallas kernels for 0% -> 0%
where the time goes in v1:
time: 883 us; the launch traced here: 873 us
  waiting for transfers between devices  400 us (45%)
  other arithmetic  173 us (20%)
  local copies, waits for them, and re-layouts  150 us (17%)
  starting transfers between devices  69.7 us (8%)
  matrix products  66.5 us (8%)
  between operations  14.5 us (2%)
    all_to_all x2, waiting for transfers between devices, return_blocks(): lax.all_to_all(buffer, ('group', 'member'), split_axis=0, concat_axis=0,...  217 us
    all_to_all x2, waiting for transfers between devices, carry_blocks(): lax.all_to_all(buffer, ('group', 'member'), split_axis=0, concat_axis=0,...  182 us
    scatter-add x2, other arithmetic, apply_graph(): total = jax.ops.segment_sum(products, segment_ids, num_segments=own_blocks)  111 us
    concatenate x2, local copies, waits for them, and re-layouts, apply_graph(): products = jnp.concatenate([to_home, to_near, to_home_r], axis=0)  49.5 us
    all_to_all x2, starting transfers between devices, carry_blocks(): lax.all_to_all(buffer, ('group', 'member'), split_axis=0, concat_axis=0,...  30.3 us
    concatenate x2, other arithmetic, apply_graph(): products = jnp.concatenate([to_home, to_near, to_home_r], axis=0)  28.8 us
    all_to_all x2, starting transfers between devices, return_blocks(): lax.all_to_all(buffer, ('group', 'member'), split_axis=0, concat_axis=0,...  27.4 us
    scatter x2, local copies, waits for them, and re-layouts, apply_graph(): jnp.zeros((device_count, BLOCK, F), jnp.bfloat16).at[target_dev].set(to_far)  24.2 us
  transfers between devices with their start and end apart: 6, of which 4 were waited for; matrix products, arithmetic and copies ran while one was open for 28% of the time, Pallas kernels for 0%

profile of v1, /device:TPU:1, one launch (start us, length us, event | category | flops | bytes accessed | tf_op | source)
XLA Modules:
  0.0 873.0 jit_solution(14968029860256077165)
XLA Ops:
  7.2 0.0 copy-start
  7.2 0.8 and_select_fusion
  8.0 0.8 scatter_custom_fusion
  8.8 0.7 copy.50
  9.5 11.5 %all-to-all-start = ((s32[128,1,1]{2,1,0:T(1,128)}), s32[128,1,1]{2,1,0:T(1,128)S(1)}, u32[]{:S(2)}, u32[]{:S(2)}) async-start(s32[128,1,1]{2,1,0:T(1,128)} %copy.50), calls=%async_computation | async-start | bytes 131072 | tf_op jit(solution)/shard_map/all_to_all | solution.py:41
  21.0 0.7 compare_select_fusion.3
  21.7 4.0 gather_fusion
  25.7 6.1 convert_bitcast_fusion.1
  31.8 6.4 copy.52
  38.2 4.3 broadcast.61.clone
  42.4 12.1 %scatter_fusion = bf16[128,128,256]{2,1,0:T(8,128)(2,1)} fusion(bf16[128,128,256]{2,1,0:T(8,128)(2,1)} %broadcast.61.clone, s32[64]{0:T(128)S(1)} %get-tuple-element.8, bf16[64,128,256]{2,1,0:T(8,128)(2,1)} %copy.52), kind=kCustom, calls=%fused_computation.11 | custom fusion | bytes 12583168 | tf_op jit(solution)/shard_map/scatter | solution.py:52
  54.5 10.3 %all-to-all-start.1 = ((bf16[128,128,256]{2,1,0:T(8,128)(2,1)}), bf16[128,128,256]{2,1,0:T(8,128)(2,1)}, u32[]{:S(2)}, u32[]{:S(2)}) async-start(bf16[128,128,256]{2,1,0:T(8,128)(2,1)} %scatter_fusion), calls=%async_computation.1 | async-start | bytes 16777216 | tf_op jit(solution)/shard_map/all_to_all | solution.py:21
  64.8 4.6 clamp_reduce_fusion
  69.5 6.5 gather_fusion.3
  75.9 100.2 %all-to-all-done.1 = bf16[128,128,256]{2,1,0:T(8,128)(2,1)} async-done(((bf16[128,128,256]{2,1,0:T(8,128)(2,1)}), bf16[128,128,256]{2,1,0:T(8,128)(2,1)}, u32[]{:S(2)}, u32[]{:S(2)}) %all-to-all-start.1) | async-done | bytes 8388640 | tf_op jit(solution)/shard_map/all_to_all | solution.py:21
  176.2 15.1 %all-to-all-start.2 = ((bf16[128,128,256]{2,1,0:T(8,128)(2,1)}), bf16[128,128,256]{2,1,0:T(8,128)(2,1)}, u32[]{:S(2)}, u32[]{:S(2)}) async-start(bf16[128,128,256]{2,1,0:T(8,128)(2,1)} %gather_fusion.3), calls=%async_computation.2 | async-start | bytes 16777216 | tf_op jit(solution)/shard_map/all_to_all | solution.py:17
  191.2 0.5 all-gather.3.cloned.1.call-start
  191.8 0.0 copy-start.9
  191.8 2.9 gather_fusion.2
  194.7 2.8 gather_fusion.1
  197.5 0.1 pad_add_fusion
  197.6 6.9 convolution_bitcast_fusion.4
  204.4 4.5 convolution_bitcast_fusion.5
  208.9 7.9 fusion.2
  216.9 2.5 copy.57
  219.4 83.2 %all-to-all-done.2 = bf16[128,128,256]{2,1,0:T(8,128)(2,1)} async-done(((bf16[128,128,256]{2,1,0:T(8,128)(2,1)}), bf16[128,128,256]{2,1,0:T(8,128)(2,1)}, u32[]{:S(2)}, u32[]{:S(2)}) %all-to-all-start.2) | async-done | bytes 8388640 | tf_op jit(solution)/shard_map/all_to_all | solution.py:17
  302.6 6.1 gather_fusion.4
  308.8 4.2 convolution_bitcast_fusion.3
  312.9 15.9 %pad_maximum_fusion = f32[192,128,256]{1,2,0:T(8,128)} fusion(f32[64,128,256]{1,2,0:T(8,128)S(1)} %convolution_bitcast_fusion.3, f32[64,128,256]{1,2,0:T(8,128)} %convolution_bitcast_fusion.4, f32[64,128,256]{1,2,0:T(8,128)} %convolution_bitcast_fusion.5), kind=kLoop, calls=%fused_computation.15 | loop fusion | flops 12582912 | bytes 50331648 | tf_op jit(solution)/shard_map/concatenate | solution.py:64
  328.9 24.6 %copy.58 = f32[192,128,256]{2,1,0:T(8,128)} copy(f32[192,128,256]{1,2,0:T(8,128)} %pad_maximum_fusion) | data formatting | bytes 50331648 | tf_op jit(solution)/shard_map/concatenate | solution.py:64
  353.5 55.0 %scatter_fusion.1 = f32[16,128,256]{2,1,0:T(8,128)} fusion(f32[16,128,256]{2,1,0:T(8,128)} %copy.57, s32[192]{0:T(256)S(1)} %pad_add_fusion, f32[192,128,256]{2,1,0:T(8,128)} %copy.58), kind=kCustom, calls=%fused_computation.12 | custom fusion | flops 6291456 | bytes 75498240 | tf_op jit(solution)/shard_map/scatter-add | solution.py:65
  408.5 1.7 convert_element_type.31
  410.3 3.5 multiply_convert_fusion
  413.8 1.0 copy-done.6
  414.7 1.5 fusion.4
  416.3 0.0 all-gather.3.cloned.1.call-update
  416.3 2.0 fusion.16
  418.3 1.9 copy-done.3
  420.2 0.1 slice.33
  420.4 6.5 gather_fusion.8
  426.9 15.2 %all-to-all-start.4 = ((bf16[128,128,256]{2,1,0:T(8,128)(2,1)}), bf16[128,128,256]{2,1,0:T(8,128)(2,1)}, u32[]{:S(2)}, u32[]{:S(2)}) async-start(bf16[128,128,256]{2,1,0:T(8,128)(2,1)} %gather_fusion.8), calls=%async_computation.4 | async-start | bytes 16777216 | tf_op jit(solution)/shard_map/all_to_all | solution.py:17
  442.1 2.8 gather_fusion.5
  444.9 6.1 convert_bitcast_fusion
  451.1 6.4 copy.60
  457.4 4.2 broadcast.61
  461.7 12.2 %scatter_fusion.2 = bf16[128,128,256]{2,1,0:T(8,128)(2,1)} fusion(bf16[128,128,256]{2,1,0:T(8,128)(2,1)} %broadcast.61, s32[64]{0:T(128)S(1)} %get-tuple-element.8, bf16[64,128,256]{2,1,0:T(8,128)(2,1)} %copy.60), kind=kCustom, calls=%fused_computation.13 | custom fusion | bytes 12583168 | tf_op jit(solution)/shard_map/scatter | solution.py:52
  473.9 99.2 %all-to-all-done.4 = bf16[128,128,256]{2,1,0:T(8,128)(2,1)} async-done(((bf16[128,128,256]{2,1,0:T(8,128)(2,1)}), bf16[128,128,256]{2,1,0:T(8,128)(2,1)}, u32[]{:S(2)}, u32[]{:S(2)}) %all-to-all-start.4) | async-done | bytes 8388640 | tf_op jit(solution)/shard_map/all_to_all | solution.py:17
  573.1 17.2 %all-to-all-start.3 = ((bf16[128,128,256]{2,1,0:T(8,128)(2,1)}), bf16[128,128,256]{2,1,0:T(8,128)(2,1)}, u32[]{:S(2)}, u32[]{:S(2)}) async-start(bf16[128,128,256]{2,1,0:T(8,128)(2,1)} %scatter_fusion.2), calls=%async_computation.3 | async-start | bytes 16777216 | tf_op jit(solution)/shard_map/all_to_all | solution.py:21
  590.3 3.6 gather_fusion.7
  593.9 2.8 gather_fusion.6
  596.6 6.9 convolution_bitcast_fusion.2
  603.6 4.5 convolution_bitcast_fusion.1
  608.1 6.2 gather_fusion.9
  614.2 4.4 convolution_bitcast_fusion
  618.7 1.0 copy-done.2
  619.7 12.8 %pad_maximum_fusion.1 = f32[192,128,256]{1,2,0:T(8,128)} fusion(f32[64,128,256]{1,2,0:T(8,128)S(1)} %convolution_bitcast_fusion, f32[64,128,256]{1,2,0:T(8,128)S(1)} %copy-done.2, f32[64,128,256]{1,2,0:T(8,128)} %convolution_bitcast_fusion.2), kind=kLoop, calls=%fused_computation.16 | loop fusion | flops 12582912 | bytes 50331648 | tf_op jit(solution)/shard_map/concatenate | solution.py:64
  632.6 24.8 %copy.66 = f32[192,128,256]{2,1,0:T(8,128)} copy(f32[192,128,256]{1,2,0:T(8,128)} %pad_maximum_fusion.1) | data formatting | bytes 50331648 | tf_op jit(solution)/shard_map/concatenate | solution.py:64
  657.4 116.9 %all-to-all-done.3 = bf16[128,128,256]{2,1,0:T(8,128)(2,1)} async-done(((bf16[128,128,256]{2,1,0:T(8,128)(2,1)}), bf16[128,128,256]{2,1,0:T(8,128)(2,1)}, u32[]{:S(2)}, u32[]{:S(2)}) %all-to-all-start.3) | async-done | bytes 8388640 | tf_op jit(solution)/shard_map/all_to_all | solution.py:21
  774.3 7.9 fusion
  782.2 2.5 copy.65
  784.8 55.6 %scatter_fusion.3 = f32[16,128,256]{2,1,0:T(8,128)} fusion(f32[16,128,256]{2,1,0:T(8,128)} %copy.65, s32[192]{0:T(256)S(1)} %pad_add_fusion, f32[192,128,256]{2,1,0:T(8,128)} %copy.66), kind=kCustom, calls=%fused_computation.14 | custom fusion | flops 6291456 | bytes 75498240 | tf_op jit(solution)/shard_map/scatter-add | solution.py:65
  840.4 3.8 slice_add_fusion
  844.2 20.9 %reduce_sum.9 = f32[512,256]{1,0:T(8,128)S(1)} reduce(f32[128,512,256]{2,1,0:T(8,128)} %bitcast.9, f32[]{:T(128)} %constant.44.clone.1), dimensions={0}, to_apply=%region_3.4 | reduce | flops 16646144 | bytes 67633152 | tf_op jit(solution)/shard_map/reduce_sum | solution.py:81
  865.1 0.8 broadcast_multiply_fusion
  (27 shorter events, 0.1 us)
Async XLA Ops:
  7.2 190.4 %copy-start = (bf16[64,128,128]{2,1,0:T(8,128)(2,1)S(1)}, bf16[64,128,128]{2,1,0:T(8,128)(2,1)}, u32[]{:S(2)}) copy-start(bf16[64,128,128]{2,1,0:T(8,128)(2,1)} %param.12) | copy-start | bytes 6291460
  9.5 45.0 %all-to-all-start = ((s32[128,1,1]{2,1,0:T(1,128)}), s32[128,1,1]{2,1,0:T(1,128)S(1)}, u32[]{:S(2)}, u32[]{:S(2)}) async-start(s32[128,1,1]{2,1,0:T(1,128)} %copy.50), calls=%async_computation | async-start | bytes 131072 | tf_op jit(solution)/shard_map/all_to_all | solution.py:41
  54.5 14.9 %copy-start.1 = (bf16[2048,256]{1,0:T(8,128)(2,1)S(1)}, bf16[2048,256]{1,0:T(8,128)(2,1)}, u32[]{:S(2)}) copy-start(bf16[2048,256]{1,0:T(8,128)(2,1)} %param.9) | copy-start | bytes 3145732
  54.5 121.7 %all-to-all-start.1 = ((bf16[128,128,256]{2,1,0:T(8,128)(2,1)}), bf16[128,128,256]{2,1,0:T(8,128)(2,1)}, u32[]{:S(2)}, u32[]{:S(2)}) async-start(bf16[128,128,256]{2,1,0:T(8,128)(2,1)} %scatter_fusion), calls=%async_computation.1 | async-start | bytes 16777216 | tf_op jit(solution)/shard_map/all_to_all | solution.py:21
  75.9 115.8 %copy-start.10 = (s32[64]{0:T(128)S(1)}, s32[64]{0:T(128)}, u32[]{:S(2)}) copy-start(s32[64]{0:T(128)} %param.10) | copy-start | bytes 772
  176.2 126.4 %all-to-all-start.2 = ((bf16[128,128,256]{2,1,0:T(8,128)(2,1)}), bf16[128,128,256]{2,1,0:T(8,128)(2,1)}, u32[]{:S(2)}, u32[]{:S(2)}) async-start(bf16[128,128,256]{2,1,0:T(8,128)(2,1)} %gather_fusion.3), calls=%async_computation.2 | async-start | bytes 16777216 | tf_op jit(solution)/shard_map/all_to_all | solution.py:17
  191.2 653.0 %all-gather.3.cloned.1.call-start = ((), (), s32[]{:S(2)}) async-start(), calls=%async_computation.5 | async-start | bytes 67633152 | tf_op jit(solution)/shard_map/all_gather | solution.py:81
  191.8 2.9 copy-start.9
  194.7 2.8 copy-start.8
  197.6 6.9 copy-start.5
  353.5 56.8 %copy-start.7 = (bf16[512,256]{1,0:T(8,128)(2,1)S(1)}, bf16[512,256]{1,0:T(8,128)(2,1)}, u32[]{:S(2)}) copy-start(bf16[512,256]{1,0:T(8,128)(2,1)} %param.16) | copy-start | bytes 786436
  413.8 1.0 copy-start.6
  418.3 1.9 copy-start.3
  426.9 146.2 %all-to-all-start.4 = ((bf16[128,128,256]{2,1,0:T(8,128)(2,1)}), bf16[128,128,256]{2,1,0:T(8,128)(2,1)}, u32[]{:S(2)}, u32[]{:S(2)}) async-start(bf16[128,128,256]{2,1,0:T(8,128)(2,1)} %gather_fusion.8), calls=%async_computation.4 | async-start | bytes 16777216 | tf_op jit(solution)/shard_map/all_to_all | solution.py:17
  573.1 201.2 %all-to-all-start.3 = ((bf16[128,128,256]{2,1,0:T(8,128)(2,1)}), bf16[128,128,256]{2,1,0:T(8,128)(2,1)}, u32[]{:S(2)}, u32[]{:S(2)}) async-start(bf16[128,128,256]{2,1,0:T(8,128)(2,1)} %scatter_fusion.2), calls=%async_computation.3 | async-start | bytes 16777216 | tf_op jit(solution)/shard_map/all_to_all | solution.py:21
  596.6 6.9 copy-start.4
  614.2 5.5 copy-start.2
Sparse Core Ops, SparseCore 0:
  416.4 360.2 all-gather.2
